TPU v7x, 32 devices: a whole 2x2x4 slice. The times are simulated.
32 devices in a mesh: seq: 8 (over y, x, core), head: 4 (over z).
Axes of the slice: x: 2, y: 2, z: 4, core: 2. Of those that a mesh axis runs over, the one named last changes fastest.
Arguments:
- queries: bfloat16 [4096, 4096], P('seq', 'head'), may hold values from -6 to 6
- keys: bfloat16 [4096, 4096], P('seq', 'head'), may hold values from -6 to 6
- values: bfloat16 [4096, 4096], P('seq', 'head'), may hold values from -48 to 48
- gate_logits: bfloat16 [4096, 4096], P('seq', 'head'), may hold values from -8 to 8
- out_weight: bfloat16 [4096, 6144], P('head'), may hold values from -0.125 to 0.125
Outputs:
- layer_out: bfloat16 [4096, 6144], P('seq', 'head')
All inputs are finite; a program needn't handle non-finite values.
Results may differ from a plain program's by a relative error of at most 0.02.
Values may be sent and summed in bfloat16 or wider, within the bound.
No kernel may reach another device: no remote copies, remote signals or barrier semaphores. Data moves between devices by JAX's collectives and lax.ppermute only.
A program may use at most 64 MiB of HBM per device.

v0:
```python
import jax
import jax.numpy as jnp
from jax import lax
from jax.sharding import PartitionSpec as P

HEADS = 32
HEAD_DIM = 128


def activate(raw_input):
    return jax.nn.silu(raw_input.astype(jnp.float32)).astype(jnp.bfloat16)


def body(queries, keys, values, gate_logits, out_weight):
    tokens_here = queries.shape[0]
    feature_count = queries.shape[1]
    heads_here = feature_count // HEAD_DIM
    block_rows = min(512, tokens_here)
    block_count = tokens_here // block_rows
    shape_blocks = (block_count, block_rows, heads_here, HEAD_DIM)
    active_q = activate(queries).reshape(shape_blocks)
    active_k = activate(keys).reshape(shape_blocks)
    active_v = activate(values).reshape(shape_blocks)
    block_states = jnp.einsum(
        "nshd,nshe->nhde", active_k, active_v, preferred_element_type=jnp.float32
    )
    span_total = jnp.sum(block_states, axis=0)
    earlier_local = jnp.cumsum(block_states, axis=0) - block_states
    my_index = lax.axis_index("seq")
    shards = lax.all_gather(
        span_total[None].astype(jnp.bfloat16), "seq", axis=0, tiled=True
    ).astype(jnp.float32)
    positions = jnp.arange(shards.shape[0], dtype=jnp.int32)
    weights = (positions < my_index).astype(jnp.float32)
    prefix = jnp.zeros_like(span_total) + jnp.sum(shards * weights[:, None, None, None], axis=0)
    before = (prefix[None] + earlier_local).astype(jnp.bfloat16)
    causal_mask = jnp.tril(jnp.ones((block_rows, block_rows), jnp.float32))
    scores = jnp.einsum("nthd,nshd->nhts", active_q, active_k, preferred_element_type=jnp.float32)
    scores = (scores * causal_mask).astype(jnp.bfloat16)
    within_block = jnp.einsum(
        "nhts,nshd->nthd", scores, active_v, preferred_element_type=jnp.float32
    )
    from_state = jnp.einsum("nthd,nhde->nthe", active_q, before, preferred_element_type=jnp.float32)
    attended = (within_block + from_state).reshape(tokens_here, feature_count)
    square_sums = lax.psum(jnp.sum(attended * attended, axis=-1), "head")
    scaling = lax.rsqrt(square_sums / (HEADS * HEAD_DIM) + 1e-06)
    gate = jax.nn.sigmoid(gate_logits.astype(jnp.float32))
    normed = (attended * scaling[:, None] * gate).astype(jnp.bfloat16)
    reduced = lax.psum_scatter(
        lax.dot_general(
            out_weight, normed, (((0,), (1,)), ((), ())), preferred_element_type=jnp.float32
        ).astype(jnp.bfloat16),
        "head",
        scatter_dimension=0,
        tiled=True,
    ).astype(jnp.float32)
    return reduced.T.astype(jnp.bfloat16)


def solution(mesh):
    return jax.shard_map(
        body,
        mesh=mesh,
        in_specs=(
            P("seq", "head"),
            P("seq", "head"),
            P("seq", "head"),
            P("seq", "head"),
            P("head", None),
        ),
        out_specs=P("seq", "head"),
        check_vma=False,
    )
```

profile of v0, /device:TPU:0, one launch (start us, length us, event | category | flops | bytes accessed | tf_op | source)
XLA Modules:
  0.0 192.8 jit_solution(12036253391915671986)
XLA Ops:
  6.5 0.0 copy-start
  6.5 0.0 all-gather.3.cloned.1.call-start
  6.5 1.9 fusion.17
  8.5 0.5 copy.19
  9.0 0.0 copy-done
  9.0 1.8 fusion.38
  10.8 0.0 copy-start.1
  10.8 0.0 copy-start.2
  10.8 0.0 all-gather.3.cloned.1.call-update
  10.8 0.0 reduce-scatter.2.cloned.1.call-start
  10.9 1.1 fusion.31
  12.0 29.5 %all-gather.3.cloned.1.call-done = bf16[64,128,128]{2,1,0:T(8,128)(2,1)} async-done(((bf16[8,128,128]{2,1,0:T(8,128)(2,1)}), bf16[64,128,128]{2,1,0:T(8,128)(2,1)}) %all-gather.3.cloned.1.call-update) | async-done | bytes 2097168 | tf_op jit(solution)/shard_map/all_gather | solution.py:30
  41.5 2.1 %fusion.2 = f32[8,128,128]{2,1,0:T(8,128)S(1)} fusion(bf16[8,8,128,128]{3,2,1,0:T(8,128)(2,1)} %bitcast.47, f32[8]{0:T(128)S(1)} %compare_convert_fusion), kind=kLoop, calls=%fused_computation.5 | loop fusion | flops 3014656 | bytes 2621472 | tf_op jit(solution)/shard_map/reduce_sum | solution.py:35
  43.6 0.0 copy-done.1
  43.6 0.0 copy-done.2
  43.6 2.2 %fusion.24 = f32[8,128,512]{2,1,0:T(8,128)} fusion(f32[8,128,128]{2,1,0:T(8,128)S(1)} %fusion.2, f32[8,128,128]{2,1,0:T(8,128)S(1)} %copy-done.2, bf16[512,1024]{1,0:T(8,128)(2,1)S(1)} %copy-done.1), kind=kOutput, calls=%fused_computation.33 | convolution fusion | flops 137756672 | bytes 4194304 | tf_op jit(solution)/shard_map/nthd,nhde->nthe/dot_general | solution.py:43
  45.8 5.3 %fusion.18 = (f32[512]{0:T(512)S(1)}, f32[8,128,512]{2,1,0:T(8,128)S(1)}) fusion(f32[8,128,512]{2,1,0:T(8,128)} %fusion.24, f32[512,512]{1,0:T(8,128)} %fusion.31, bf16[512,8,128]{0,2,1:T(8,128)(2,1)S(1)} %bitcast.50, bf16[512,1024]{1,0:T(8,128)(2,1)} %param.7, bf16[512,1024]{1,0:T(8,128)(2,1)} %param.5), kind=kOutput, calls=%fused_computation.27 | convolution fusion | flops 1085799936 | bytes 8390656 | tf_op jit(solution)/shard_map/nhts,nshd->nthd/dot_general | solution.py:40
  51.1 11.7 %psum.7 = f32[512]{0:T(512)S(1)} all-reduce(f32[512]{0:T(512)S(1)} %get-tuple-element.7), channel_id=1, replica_groups=mesh['seq'=8,'head'=4] {'head'}, use_global_device_ids=true, to_apply=%region_2.3 | all-reduce | flops 512 | bytes 4096 | tf_op jit(solution)/shard_map/psum | solution.py:45
  62.8 1.8 copy.17
  64.6 13.1 %fusion = bf16[6144,512]{0,1:T(8,128)(2,1)} fusion(bf16[1024,6144]{1,0:T(8,128)(2,1)} %param.9, bf16[512,1024]{1,0:T(8,128)(2,1)} %param.8, f32[512,1024]{1,0:T(8,128)} %copy.17, f32[512]{0:T(512)S(1)} %add_rsqrt_fusion), kind=kOutput, calls=%fused_computation.2 | convolution fusion | flops 6449266688 | bytes 22022144 | tf_op jit(solution)/shard_map/dot_general | solution.py:50
  77.8 0.0 reduce-scatter.2.cloned.1.call-update
  77.8 108.2 %reduce-scatter.2.cloned.1.call-done = bf16[1536,512]{0,1:T(8,128)(2,1)} async-done(((bf16[6144,512]{0,1:T(8,128)(2,1)}), bf16[1536,512]{0,1:T(8,128)(2,1)}) %reduce-scatter.2.cloned.1.call-update) | async-done | bytes 1572880 | tf_op jit(solution)/shard_map/reduce_scatter | solution.py:49
  (2 shorter events, 0.0 us)
Async XLA Ops:
  6.5 2.5 %copy-start = (bf16[512,1024]{1,0:T(8,128)(2,1)S(1)}, bf16[512,1024]{1,0:T(8,128)(2,1)}, u32[]{:S(2)}) copy-start(bf16[512,1024]{1,0:T(8,128)(2,1)} %param.7) | copy-start | bytes 3145732
  6.5 34.9 %all-gather.3.cloned.1.call-start = ((), (), s32[]{:S(2)}) async-start(), calls=%async_computation.2 | async-start | bytes 2359296 | tf_op jit(solution)/shard_map/all_gather | solution.py:30
  10.8 32.8 %copy-start.1 = (bf16[512,1024]{1,0:T(8,128)(2,1)S(1)}, bf16[512,1024]{1,0:T(8,128)(2,1)}, u32[]{:S(2)}) copy-start(bf16[512,1024]{1,0:T(8,128)(2,1)} %param.5) | copy-start | bytes 3145732
  10.8 32.8 %copy-start.2 = (f32[8,128,128]{2,1,0:T(8,128)S(1)}, f32[8,128,128]{2,1,0:T(8,128)}, u32[]{:S(2)}) copy-start(f32[8,128,128]{2,1,0:T(8,128)} %get-tuple-element.6) | copy-start | bytes 1572868
  10.8 175.1 %reduce-scatter.2.cloned.1.call-start = ((), (), s32[]{:S(2)}) async-start(), calls=%async_computation.1 | async-start | bytes 7864320 | tf_op jit(solution)/shard_map/reduce_scatter | solution.py:49
Sparse Core Ops, SparseCore 0:
  10.9 30.4 all-gather.2
  77.9 107.9 reduce-scatter.1
where the time goes:
time: 193 us
  waiting for transfers between devices  138 us (72%)
  matrix products  22.3 us (12%)
  between operations  13.5 us (7%)
  blocking collectives  11.7 us (6%)
  other arithmetic  5.15 us (3%)
  local copies, waits for them, and re-layouts  2.39 us (1%)
    reduce_scatter x1, waiting for transfers between devices, body(): lax.psum_scatter(lax.dot_general(out_weight, normed, (((0,), (1,)), ((),...  108 us
    all_gather x1, waiting for transfers between devices, body(): lax.all_gather(span_total[None].astype(jnp.bfloat16), 'seq', axis=0, tile...  29.5 us
    dot_general x1, matrix products, body(): lax.dot_general(out_weight, normed, (((0,), (1,)), ((), ())), preferred_e...  13.1 us
    psum x1, blocking collectives, body(): square_sums = lax.psum(jnp.sum(attended * attended, axis=-1), 'head')  11.7 us
    dot_general x1, matrix products, body(): jnp.einsum('nhts,nshd->nthd', scores, active_v, preferred_element_type=jn...  5.26 us
  transfers between devices with their start and end apart: 2, of which 2 were waited for; matrix products, arithmetic and copies ran while one was open for 1% of the time, Pallas kernels for 0%

commit v1 on v0

--- a/solution.py
+++ b/solution.py
@@ -27,9 +27,29 @@
     span_total = jnp.sum(block_states, axis=0)
     earlier_local = jnp.cumsum(block_states, axis=0) - block_states
     my_index = lax.axis_index("seq")
-    shards = lax.all_gather(
-        span_total[None].astype(jnp.bfloat16), "seq", axis=0, tiled=True
-    ).astype(jnp.float32)
+
+    def _pack_desk(panel):
+        named_axis = "seq"
+        workers = lax.axis_size(named_axis)
+        y2 = map(lambda num: (num, (num + 1) % workers), range(workers))
+        piece_next = range(workers)
+        long_array = map(lambda num: (num, (num - 1) % workers), piece_next)
+        rows = list(y2)
+        extra, top = ([panel], [panel])
+        found = list(long_array)
+        for _ in range(workers // 2):
+            arr_now = lax.ppermute(extra[-1], named_axis, rows)
+            extra.append(arr_now)
+        for _ in [*range((workers - 1) // 2)]:
+            lower = lax.ppermute(top[-1], named_axis, found)
+            top.append(lower)
+        mid_arr = jnp.concatenate([*extra[::-1], *top[1:]], axis=0)
+        d_next = jnp.roll(
+            mid_arr, (lax.axis_index(named_axis) - workers // 2) * panel.shape[0], axis=0
+        )
+        return d_next
+
+    shards = _pack_desk(span_total[None].astype(jnp.bfloat16)).astype(jnp.float32)
     positions = jnp.arange(shards.shape[0], dtype=jnp.int32)
     weights = (positions < my_index).astype(jnp.float32)
     prefix = jnp.zeros_like(span_total) + jnp.sum(shards * weights[:, None, None, None], axis=0)

time: 193 us -> 197 us (1.021)
  waiting for transfers between devices: 138 us -> 127 us
  starting transfers between devices: 0.04 us -> 8.58 us
  local copies, waits for them, and re-layouts: 2.39 us -> 8.82 us
  blocking collectives: 11.7 us -> 14.2 us
  other arithmetic: 5.15 us -> 2.67 us
    all_gather x1 -> x0, waiting for transfers between devices: 29.5 us -> none  [body(): lax.all_gather(span_total[None].astype(jnp.bfloat16), 'seq', axis=0, tile...]
    ppermute x0 -> x7, waiting for transfers between devices: none -> 18.7 us  [the longest x4 17.8 us: _pack_desk(): arr_now = lax.ppermute(extra[-1], named_axis, rows)]
    ppermute x0 -> x7, starting transfers between devices: none -> 8.58 us  [the longest x3 8.02 us: _pack_desk(): lower = lax.ppermute(top[-1], named_axis, found)]
    unnamed x6 -> x19, local copies, waits for them, and re-layouts: 0.01 us -> 6.32 us
    psum x1, blocking collectives: 11.7 us -> 14.2 us  [body(): square_sums = lax.psum(jnp.sum(attended * attended, axis=-1), 'head')]
  transfers between devices with their start and end apart: 2 -> 8, of which waited for: 2 -> 5; matrix products, arithmetic and copies ran while one was open for 1% -> 5% of each run, Pallas kernels for 0% -> 0%
where the time goes in v1:
time: 197 us; the launch traced here: 196 us
  waiting for transfers between devices  127 us (64%)
  matrix products  21.1 us (11%)
  blocking collectives  14.2 us (7%)
  between operations  13.6 us (7%)
  local copies, waits for them, and re-layouts  8.82 us (4%)
  starting transfers between devices  8.58 us (4%)
  other arithmetic  2.67 us (1%)
    reduce_scatter x1, waiting for transfers between devices, body(): lax.psum_scatter(lax.dot_general(out_weight, normed, (((0,), (1,)), ((),...  108 us
    ppermute x4, waiting for transfers between devices, _pack_desk(): arr_now = lax.ppermute(extra[-1], named_axis, rows)  17.8 us
    psum x1, blocking collectives, body(): square_sums = lax.psum(jnp.sum(attended * attended, axis=-1), 'head')  14.2 us
    dot_general x1, matrix products, body(): lax.dot_general(out_weight, normed, (((0,), (1,)), ((), ())), preferred_e...  12.4 us
    ppermute x3, starting transfers between devices, _pack_desk(): lower = lax.ppermute(top[-1], named_axis, found)  8.02 us
    unnamed x19, local copies, waits for them, and re-layouts  6.32 us
    dot_general x1, matrix products, body(): jnp.einsum('nhts,nshd->nthd', scores, active_v, preferred_element_type=jn...  5.6 us
  transfers between devices with their start and end apart: 8, of which 5 were waited for; matrix products, arithmetic and copies ran while one was open for 5% of the time, Pallas kernels for 0%

profile of v1, /device:TPU:0, one launch (start us, length us, event | category | flops | bytes accessed | tf_op | source)
XLA Modules:
  0.0 196.2 jit_solution(545238483701542012)
XLA Ops:
  6.5 1.9 fusion.16
  8.5 0.5 copy.13
  9.0 0.8 fusion.24
  9.9 0.5 collective-permute-start
  10.5 6.9 %collective-permute-done = bf16[1,8,128,128]{3,2,1,0:T(8,128)(2,1)S(1)} collective-permute-done((bf16[1,8,128,128]{3,2,1,0:T(8,128)(2,1)S(1)}, bf16[1,8,128,128]{3,2,1,0:T(8,128)(2,1)S(1)}, u32[]{:S(2)}, u32[]{:S(2)}) %collective-permute-start) | collective-permute-done | bytes 262176 | tf_op jit(solution)/shard_map/ppermute | solution.py:41
  17.4 0.0 collective-permute-start.1
  17.4 2.6 %collective-permute-start.4 = (bf16[1,8,128,128]{3,2,1,0:T(8,128)(2,1)S(1)}, bf16[1,8,128,128]{3,2,1,0:T(8,128)(2,1)S(1)}, u32[]{:S(2)}, u32[]{:S(2)}) collective-permute-start(bf16[1,8,128,128]{3,2,1,0:T(8,128)(2,1)S(1)} %convert_bitcast_fusion), channel_id=1, source_target_pairs={{0,28},{4,0},{8,4},{12,8},{16,12},{20,16},{24,20},{28,24},{1,29},{... | collective-permute-start | bytes 786440 | tf_op jit(solution)/shard_map/ppermute | solution.py:44
  20.0 5.2 %collective-permute-done.1 = bf16[1,8,128,128]{3,2,1,0:T(8,128)(2,1)S(1)} collective-permute-done((bf16[1,8,128,128]{3,2,1,0:T(8,128)(2,1)S(1)}, bf16[1,8,128,128]{3,2,1,0:T(8,128)(2,1)S(1)}, u32[]{:S(2)}, u32[]{:S(2)}) %collective-permute-start.1) | collective-permute-done | bytes 262176 | tf_op jit(solution)/shard_map/ppermute | solution.py:41
  25.2 0.1 fusion.28
  25.3 2.7 %collective-permute-start.5 = (bf16[1,8,128,128]{3,2,1,0:T(8,128)(2,1)S(1)}, bf16[1,8,128,128]{3,2,1,0:T(8,128)(2,1)}, u32[]{:S(2)}, u32[]{:S(2)}) collective-permute-start(bf16[1,8,128,128]{3,2,1,0:T(8,128)(2,1)S(1)} %collective-permute-done.4), channel_id=1, source_target_pairs={{0,28},{4,0},{8,4},{12,8},{16,12},{20,16},{24,20},{28,24},{1,29},{... | collective-permute-start | bytes 786440 | tf_op jit(solution)/shard_map/ppermute | solution.py:44
  28.0 5.7 %collective-permute-done.2 = bf16[1,8,128,128]{3,2,1,0:T(8,128)(2,1)} collective-permute-done((bf16[1,8,128,128]{3,2,1,0:T(8,128)(2,1)S(1)}, bf16[1,8,128,128]{3,2,1,0:T(8,128)(2,1)}, u32[]{:S(2)}, u32[]{:S(2)}) %collective-permute-start.2) | collective-permute-done | bytes 262176 | tf_op jit(solution)/shard_map/ppermute | solution.py:41
  33.7 0.0 collective-permute-start.3
  33.7 5.6 %fusion.1 = f32[8,128,512]{2,1,0:T(8,128)} fusion(f32[512,512]{1,0:T(8,128)S(1)} %fusion.28, bf16[512,8,128]{0,2,1:T(8,128)(2,1)S(1)} %bitcast.49, bf16[512,1024]{1,0:T(8,128)(2,1)} %param.7, bf16[512,1024]{1,0:T(8,128)(2,1)} %param.5), kind=kOutput, calls=%fused_computation.3 | convolution fusion | flops 1084227584 | bytes 6291456 | tf_op jit(solution)/shard_map/nhts,nshd->nthd/dot_general | solution.py:60
  39.3 0.0 collective-permute-done.5
  39.3 2.7 %collective-permute-start.6 = (bf16[1,8,128,128]{3,2,1,0:T(8,128)(2,1)}, bf16[1,8,128,128]{3,2,1,0:T(8,128)(2,1)S(1)}, u32[]{:S(2)}, u32[]{:S(2)}) collective-permute-start(bf16[1,8,128,128]{3,2,1,0:T(8,128)(2,1)} %collective-permute-done.5), channel_id=1, source_target_pairs={{0,28},{4,0},{8,4},{12,8},{16,12},{20,16},{24,20},{28,24},{1,29},{... | collective-permute-start | bytes 786440 | tf_op jit(solution)/shard_map/ppermute | solution.py:44
  42.0 1.0 constant_dynamic-update-slice_fusion.15
  43.0 1.0 constant_dynamic-update-slice_fusion.14
  44.1 0.1 constant_dynamic-update-slice_fusion.11
  44.2 0.0 copy-start.1
  44.2 1.1 constant_dynamic-update-slice_fusion.9
  45.3 0.9 collective-permute-done.6
  46.3 1.0 constant_dynamic-update-slice_fusion.7
  47.2 1.0 constant_dynamic-update-slice_fusion.6
  48.3 0.1 constant_dynamic-update-slice_fusion.3
  48.4 1.0 constant_dynamic-update-slice_fusion.1
  49.5 0.5 multiply_reduce_fusion
  50.0 2.3 %fusion.17 = (f32[512]{0:T(512)S(1)}, f32[8,128,512]{2,1,0:T(8,128)}) fusion(f32[8,128,512]{2,1,0:T(8,128)S(1)} %copy-done.2, f32[8,128,128]{2,1,0:T(8,128)S(1)} %multiply_reduce_fusion, f32[8,128,128]{2,1,0:T(8,128)S(1)} %fusion.24, bf16[512,1024]{1,0:T(8,128)(2,1)S(1)} %copy-done.1), kind=kOutput, calls=%fused_computation.26 | convolution fusion | flops 139329024 | bytes 6293504 | tf_op jit(solution)/shard_map/nthd,nhde->nthe/dot_general | solution.py:63
  52.2 1.9 copy.11
  54.2 14.2 %psum.7 = f32[512]{0:T(512)S(1)} all-reduce(f32[512]{0:T(512)S(1)} %get-tuple-element.5), channel_id=1, replica_groups=mesh['seq'=8,'head'=4] {'head'}, use_global_device_ids=true, to_apply=%region_2.3 | all-reduce | flops 512 | bytes 4096 | tf_op jit(solution)/shard_map/psum | solution.py:65
  68.4 12.4 %fusion = bf16[6144,512]{0,1:T(8,128)(2,1)} fusion(bf16[1024,6144]{1,0:T(8,128)(2,1)} %param.9, bf16[512,1024]{1,0:T(8,128)(2,1)} %param.8, f32[512,1024]{1,0:T(8,128)S(1)} %copy.11, f32[512]{0:T(512)S(1)} %add_rsqrt_fusion), kind=kOutput, calls=%fused_computation.2 | convolution fusion | flops 6449266688 | bytes 22022144 | tf_op jit(solution)/shard_map/dot_general | solution.py:70
  80.8 0.0 reduce-scatter.2.cloned.1.call-update
  80.9 108.5 %reduce-scatter.2.cloned.1.call-done = bf16[1536,512]{0,1:T(8,128)(2,1)} async-done(((bf16[6144,512]{0,1:T(8,128)(2,1)}), bf16[1536,512]{0,1:T(8,128)(2,1)}) %reduce-scatter.2.cloned.1.call-update) | async-done | bytes 1572880 | tf_op jit(solution)/shard_map/reduce_scatter | solution.py:69
  (20 shorter events, 0.4 us)
Async XLA Ops:
  6.5 2.5 %copy-start = (bf16[512,1024]{1,0:T(8,128)(2,1)S(1)}, bf16[512,1024]{1,0:T(8,128)(2,1)}, u32[]{:S(2)}) copy-start(bf16[512,1024]{1,0:T(8,128)(2,1)} %param.7) | copy-start | bytes 3145732
  6.5 182.8 %reduce-scatter.2.cloned.1.call-start = ((), (), s32[]{:S(2)}) async-start(), calls=%async_computation.1 | async-start | bytes 7864320 | tf_op jit(solution)/shard_map/reduce_scatter | solution.py:69
  9.9 7.5 %collective-permute-start = (bf16[1,8,128,128]{3,2,1,0:T(8,128)(2,1)S(1)}, bf16[1,8,128,128]{3,2,1,0:T(8,128)(2,1)S(1)}, u32[]{:S(2)}, u32[]{:S(2)}) collective-permute-start(bf16[1,8,128,128]{3,2,1,0:T(8,128)(2,1)S(1)} %convert_bitcast_fusion), channel_id=1, source_target_pairs={{0,4},{4,8},{8,12},{12,16},{16,20},{20,24},{24,28},{28,0},{1,5},{5... | collective-permute-start | bytes 786440 | tf_op jit(solution)/shard_map/ppermute | solution.py:41
  17.4 7.8 %collective-permute-start.1 = (bf16[1,8,128,128]{3,2,1,0:T(8,128)(2,1)S(1)}, bf16[1,8,128,128]{3,2,1,0:T(8,128)(2,1)S(1)}, u32[]{:S(2)}, u32[]{:S(2)}) collective-permute-start(bf16[1,8,128,128]{3,2,1,0:T(8,128)(2,1)S(1)} %collective-permute-done), channel_id=1, source_target_pairs={{0,4},{4,8},{8,12},{12,16},{16,20},{20,24},{24,28},{28,0},{1,5},{5... | collective-permute-start | bytes 786440 | tf_op jit(solution)/shard_map/ppermute | solution.py:41
  17.4 7.9 %collective-permute-start.4 = (bf16[1,8,128,128]{3,2,1,0:T(8,128)(2,1)S(1)}, bf16[1,8,128,128]{3,2,1,0:T(8,128)(2,1)S(1)}, u32[]{:S(2)}, u32[]{:S(2)}) collective-permute-start(bf16[1,8,128,128]{3,2,1,0:T(8,128)(2,1)S(1)} %convert_bitcast_fusion), channel_id=1, source_target_pairs={{0,28},{4,0},{8,4},{12,8},{16,12},{20,16},{24,20},{28,24},{1,29},{... | collective-permute-start | bytes 786440 | tf_op jit(solution)/shard_map/ppermute | solution.py:44
  25.2 8.5 %collective-permute-start.2 = (bf16[1,8,128,128]{3,2,1,0:T(8,128)(2,1)S(1)}, bf16[1,8,128,128]{3,2,1,0:T(8,128)(2,1)}, u32[]{:S(2)}, u32[]{:S(2)}) collective-permute-start(bf16[1,8,128,128]{3,2,1,0:T(8,128)(2,1)S(1)} %collective-permute-done.1), channel_id=1, source_target_pairs={{0,4},{4,8},{8,12},{12,16},{16,20},{20,24},{24,28},{28,0},{1,5},{5... | collective-permute-start | bytes 786440 | tf_op jit(solution)/shard_map/ppermute | solution.py:41
  25.3 14.0 %collective-permute-start.5 = (bf16[1,8,128,128]{3,2,1,0:T(8,128)(2,1)S(1)}, bf16[1,8,128,128]{3,2,1,0:T(8,128)(2,1)}, u32[]{:S(2)}, u32[]{:S(2)}) collective-permute-start(bf16[1,8,128,128]{3,2,1,0:T(8,128)(2,1)S(1)} %collective-permute-done.4), channel_id=1, source_target_pairs={{0,28},{4,0},{8,4},{12,8},{16,12},{20,16},{24,20},{28,24},{1,29},{... | collective-permute-start | bytes 786440 | tf_op jit(solution)/shard_map/ppermute | solution.py:44
  33.7 8.3 %collective-permute-start.3 = (bf16[1,8,128,128]{3,2,1,0:T(8,128)(2,1)}, bf16[1,8,128,128]{3,2,1,0:T(8,128)(2,1)}, u32[]{:S(2)}, u32[]{:S(2)}) collective-permute-start(bf16[1,8,128,128]{3,2,1,0:T(8,128)(2,1)} %collective-permute-done.2), channel_id=1, source_target_pairs={{0,4},{4,8},{8,12},{12,16},{16,20},{20,24},{24,28},{28,0},{1,5},{5... | collective-permute-start | bytes 786440 | tf_op jit(solution)/shard_map/ppermute | solution.py:41
  39.3 6.9 %collective-permute-start.6 = (bf16[1,8,128,128]{3,2,1,0:T(8,128)(2,1)}, bf16[1,8,128,128]{3,2,1,0:T(8,128)(2,1)S(1)}, u32[]{:S(2)}, u32[]{:S(2)}) collective-permute-start(bf16[1,8,128,128]{3,2,1,0:T(8,128)(2,1)} %collective-permute-done.5), channel_id=1, source_target_pairs={{0,28},{4,0},{8,4},{12,8},{16,12},{20,16},{24,20},{28,24},{1,29},{... | collective-permute-start | bytes 786440 | tf_op jit(solution)/shard_map/ppermute | solution.py:44
  44.2 5.8 %copy-start.1 = (bf16[512,1024]{1,0:T(8,128)(2,1)S(1)}, bf16[512,1024]{1,0:T(8,128)(2,1)}, u32[]{:S(2)}) copy-start(bf16[512,1024]{1,0:T(8,128)(2,1)} %param.5) | copy-start | bytes 3145732
  44.2 5.8 %copy-start.2 = (f32[8,128,512]{2,1,0:T(8,128)S(1)}, f32[8,128,512]{2,1,0:T(8,128)}, u32[]{:S(2)}) copy-start(f32[8,128,512]{2,1,0:T(8,128)} %fusion.1) | copy-start | bytes 6291460
Sparse Core Ops, SparseCore 0:
  81.0 108.2 reduce-scatter.1
